TPU v7x, 32 devices: a whole 2x2x4 slice. The times are simulated.
32 devices in a mesh: inl: 4 (over y, core), xl: 2 (over x), gz: 4 (over z).
Axes of the slice: x: 2, y: 2, z: 4, core: 2. Of those that a mesh axis runs over, the one named last changes fastest.
Arguments:
- wave_p: float32 [32, 32, 256], P('gz', 'inl', 'xl'), may hold values from -6 to 6
- wave_p_old: float32 [32, 32, 256], P('gz', 'inl', 'xl'), may hold values from -6 to 6
- wave_q: float32 [32, 32, 256], P('gz', 'inl', 'xl'), may hold values from -6 to 6
- wave_q_old: float32 [32, 32, 256], P('gz', 'inl', 'xl'), may hold values from -6 to 6
- courant_square: float32 [32, 32, 256], P('gz', 'inl', 'xl'), may hold values from 0.05 to 0.11
- thomsen_epsilon: float32 [32, 32, 256], P('gz', 'inl', 'xl'), may hold values from 0.1 to 0.35
- thomsen_delta: float32 [32, 32, 256], P('gz', 'inl', 'xl'), may hold values from 0.02 to 0.2
- tilt_angle: float32 [32, 32, 256], P('gz', 'inl', 'xl'), may hold values from -3.140625 to 3.140625
- azimuth: float32 [32, 32, 256], P('gz', 'inl', 'xl'), may hold values from -3.140625 to 3.140625
- shear_ratio: float32 [32, 32, 256], P('gz', 'inl', 'xl'), may hold values from 0.1 to 0.6
- damping: float32 [32, 32, 256], P('gz', 'inl', 'xl'), may hold values from 0 to 0.3
- trace_samples: float32 [8192, 256], P(('inl', 'xl', 'gz')), may hold values from -6 to 6
- resample_filter: float32 [2, 256], replicated, may hold values from -0.375 to 0.375
- line_gain: float32 [64], replicated, may hold values from 0.5 to 4
- receiver_inline: int32 [8192], P(('inl', 'xl', 'gz')), may hold values from 0 to 31, as said below
- receiver_crossline: int32 [8192], P(('inl', 'xl', 'gz')), may hold values from 0 to 255, as said below
- shot_line: int32 [8192], P(('inl', 'xl', 'gz')), may hold values from 0 to 63
Outputs:
- next_p: float32 [32, 32, 256], P('gz', 'inl', 'xl')
- next_q: float32 [32, 32, 256], P('gz', 'inl', 'xl')
- prior_p: float32 [32, 32, 256], P('gz', 'inl', 'xl')
- prior_q: float32 [32, 32, 256], P('gz', 'inl', 'xl')
Inputs may be any that keep to these rules, and one draw needn't show every extreme that they name: In each aligned block of 256 traces (the traces of one device), at most 64 traces lie in one device column (equal receiver_inline // 8 and receiver_crossline // 128); in every block some column holds exactly 64. `receiver_crossline`: see receiver_inline.
All inputs are finite; a program needn't handle non-finite values.
Results may differ from a plain program's by a relative error of at most 0.000075.
Values sent between devices are 32-bit elements; how exact they have to be, the bound alone decides.
No kernel may reach another device: no remote copies, remote signals or barrier semaphores. Data moves between devices by JAX's collectives and lax.ppermute only.
A program may use at most 64 MiB of HBM per device.

v0:
```python
import jax
import jax.numpy as jnp
from jax import lax
from jax.sharding import PartitionSpec as P

second_coef = (-205.0 / 72.0, 8.0 / 5.0, -1.0 / 5.0, 8.0 / 315.0, -1.0 / 560.0)
first_coef = (0.0, 4.0 / 5.0, -1.0 / 5.0, 4.0 / 105.0, -1.0 / 280.0)


def with_halo(block, sides, width):
    for axis, dim in sides:
        count = lax.axis_size(axis)
        forward = [(i, i + 1) for i in range(count - 1)]
        backward = [(target, source) for source, target in forward]
        low = lax.ppermute(
            lax.slice_in_dim(block, block.shape[dim] - width, None, axis=dim), axis, forward
        )
        high = lax.ppermute(lax.slice_in_dim(block, 0, width, axis=dim), axis, backward)
        block = jnp.concatenate([low, block, high], axis=dim)
    return block


def derivatives(padded):
    depth = padded.shape[-3] - 8
    across = padded.shape[-2] - 8
    along = padded.shape[-1] - 8

    def piece(dz, dx, dy):
        return padded[
            ..., 4 + dz : 4 + dz + depth, 4 + dx : 4 + dx + across, 4 + dy : 4 + dy + along
        ]

    center = piece(0, 0, 0)
    u_zz = second_coef[0] * center
    u_xx = second_coef[0] * center
    u_yy = second_coef[0] * center
    for k in range(1, 5):
        u_zz = u_zz + second_coef[k] * (piece(k, 0, 0) + piece(-k, 0, 0))
        u_xx = u_xx + second_coef[k] * (piece(0, k, 0) + piece(0, -k, 0))
        u_yy = u_yy + second_coef[k] * (piece(0, 0, k) + piece(0, 0, -k))
    grad_x = first_coef[1] * (padded[..., :, 5 : 5 + across, :] - padded[..., :, 3 : 3 + across, :])
    grad_y = first_coef[1] * (
        padded[..., :, 4 : 4 + across, 5 : 5 + along]
        - padded[..., :, 4 : 4 + across, 3 : 3 + along]
    )
    for k in range(2, 5):
        grad_x = grad_x + first_coef[k] * (
            padded[..., :, 4 + k : 4 + k + across, :] - padded[..., :, 4 - k : 4 - k + across, :]
        )
        grad_y = grad_y + first_coef[k] * (
            padded[..., :, 4 : 4 + across, 4 + k : 4 + k + along]
            - padded[..., :, 4 : 4 + across, 4 - k : 4 - k + along]
        )
    u_xy = first_coef[1] * (
        grad_x[..., 4 : 4 + depth, :, 5 : 5 + along] - grad_x[..., 4 : 4 + depth, :, 3 : 3 + along]
    )
    u_xz = first_coef[1] * (
        grad_x[..., 5 : 5 + depth, :, 4 : 4 + along] - grad_x[..., 3 : 3 + depth, :, 4 : 4 + along]
    )
    u_yz = first_coef[1] * (grad_y[..., 5 : 5 + depth, :, :] - grad_y[..., 3 : 3 + depth, :, :])
    for k in range(2, 5):
        u_xy = u_xy + first_coef[k] * (
            grad_x[..., 4 : 4 + depth, :, 4 + k : 4 + k + along]
            - grad_x[..., 4 : 4 + depth, :, 4 - k : 4 - k + along]
        )
        u_xz = u_xz + first_coef[k] * (
            grad_x[..., 4 + k : 4 + k + depth, :, 4 : 4 + along]
            - grad_x[..., 4 - k : 4 - k + depth, :, 4 : 4 + along]
        )
        u_yz = u_yz + first_coef[k] * (
            grad_y[..., 4 + k : 4 + k + depth, :, :] - grad_y[..., 4 - k : 4 - k + depth, :, :]
        )
    return (u_zz, u_xx, u_yy, u_xy, u_xz, u_yz)


def anisotropy(tilt_angle, azimuth):
    sin_t = jnp.sin(tilt_angle)
    cos_t = jnp.cos(tilt_angle)
    sin_f = jnp.sin(azimuth)
    cos_f = jnp.cos(azimuth)
    a_xx = sin_t * sin_t * cos_f * cos_f
    a_yy = sin_t * sin_t * sin_f * sin_f
    a_zz = cos_t * cos_t
    a_xy = 2.0 * sin_t * sin_t * sin_f * cos_f
    a_xz = 2.0 * sin_t * cos_t * cos_f
    a_yz = 2.0 * sin_t * cos_t * sin_f
    return (a_xx, a_yy, a_zz, a_xy, a_xz, a_yz)


def advance(padded, current, previous, fields, coefs, plane, top):
    courant, eps_field, delta_field, shear, damp = fields
    a_xx, a_yy, a_zz, a_xy, a_xz, a_yz = coefs
    u_zz, u_xx, u_yy, u_xy, u_xz, u_yz = derivatives(padded)
    h_one = a_xx * u_xx + a_yy * u_yy + a_zz * u_zz + a_xy * u_xy + a_xz * u_xz + a_yz * u_yz
    h_two = u_xx + u_yy + u_zz - h_one
    wave_a = current[0]
    wave_b = current[1]
    old_a = previous[0]
    old_b = previous[1]
    new_a = (
        2.0 * wave_a
        - old_a
        + courant * ((1.0 + 2.0 * eps_field) * h_two[0] + h_one[1] + shear * (h_one[0] - h_one[1]))
        - damp * (wave_a - old_a)
    )
    new_b = (
        2.0 * wave_b
        - old_b
        + courant
        * ((1.0 + 2.0 * delta_field) * h_two[0] + h_one[1] + shear * (h_two[1] - h_two[0]))
        - damp * (wave_b - old_b)
    )
    new_a = new_a.at[top].add(plane)
    new_b = new_b.at[top].add(plane)
    return jnp.stack([new_a, new_b])


def step_amplitudes(samples, resample_filter, line_gain, lines):
    table = jnp.arange(line_gain.shape[0], dtype=jnp.int32)
    gains = jnp.sum(jnp.where(lines[:, None] == table[None, :], line_gain[None, :], 0.0), axis=1)
    return jnp.dot(samples, resample_filter.T, precision=lax.Precision.HIGHEST) * gains[:, None]


def local(
    wave_p,
    wave_p_old,
    wave_q,
    wave_q_old,
    courant_square,
    thomsen_epsilon,
    thomsen_delta,
    tilt_angle,
    azimuth,
    shear_ratio,
    damping,
    trace_samples,
    resample_filter,
    line_gain,
    receiver_inline,
    receiver_crossline,
    shot_line,
):
    depth, inline_cells, cross_cells = wave_p.shape
    cells = inline_cells * cross_cells
    steps = resample_filter.shape[0]
    xl_count = lax.axis_size("xl")
    columns = lax.axis_size("inl") * xl_count
    capacity = 2 * trace_samples.shape[0] // columns
    owner = receiver_inline // inline_cells * xl_count + receiver_crossline // cross_cells
    local_cell = receiver_inline % inline_cells * cross_cells + receiver_crossline % cross_cells
    payload = step_amplitudes(trace_samples, resample_filter, line_gain, shot_line)
    onehot = (owner[:, None] == jnp.arange(columns, dtype=jnp.int32)[None, :]).astype(jnp.int32)
    rank = jnp.sum(jnp.cumsum(onehot, axis=0) * onehot, axis=1) - 1
    slot = owner * capacity + rank
    width = payload.shape[1]
    float_buffer = (
        jnp.zeros((columns * capacity, width), jnp.float32)
        .at[slot]
        .set(payload)
        .reshape(columns, capacity, width)
    )
    label_buffer = (
        jnp.full((columns * capacity,), -1, jnp.int32)
        .at[slot]
        .set(local_cell)
        .reshape(columns, capacity)
    )
    arrived, arrived_labels = (
        lax.all_to_all(float_buffer, ("inl", "xl"), split_axis=0, concat_axis=0, tiled=True),
        lax.all_to_all(label_buffer, ("inl", "xl"), split_axis=0, concat_axis=0, tiled=True),
    )
    amplitude = arrived.reshape(-1, width)
    flat_labels = arrived_labels.reshape(-1)
    target = jnp.where(flat_labels >= 0, flat_labels, cells)
    planes = jnp.zeros((steps, cells), jnp.float32).at[:, target].add(amplitude.T, mode="drop")
    planes = lax.psum(planes, "gz")
    surface_flag = jnp.where(lax.axis_index("gz") == 0, 1.0, 0.0).astype(jnp.float32)
    planes = planes.reshape(steps, inline_cells, cross_cells) * surface_flag
    fields = (courant_square, thomsen_epsilon, thomsen_delta, shear_ratio, damping)
    current = jnp.stack([wave_p, wave_q])
    previous = jnp.stack([wave_p_old, wave_q_old])
    coefs = anisotropy(tilt_angle, azimuth)
    for step in range(steps):
        padded = with_halo(current, (("inl", 2), ("xl", 3), ("gz", 1)), 4)
        newer = advance(padded, current, previous, fields, coefs, planes[step], 0)
        previous = current
        current = newer
    return (current[0], current[1], previous[0], previous[1])


def solution(mesh):
    return jax.shard_map(
        local,
        mesh=mesh,
        in_specs=(
            P("gz", "inl", "xl"),
            P("gz", "inl", "xl"),
            P("gz", "inl", "xl"),
            P("gz", "inl", "xl"),
            P("gz", "inl", "xl"),
            P("gz", "inl", "xl"),
            P("gz", "inl", "xl"),
            P("gz", "inl", "xl"),
            P("gz", "inl", "xl"),
            P("gz", "inl", "xl"),
            P("gz", "inl", "xl"),
            P(("inl", "xl", "gz"), None),
            P(),
            P(),
            P(("inl", "xl", "gz")),
            P(("inl", "xl", "gz")),
            P(("inl", "xl", "gz")),
        ),
        out_specs=(
            P("gz", "inl", "xl"),
            P("gz", "inl", "xl"),
            P("gz", "inl", "xl"),
            P("gz", "inl", "xl"),
        ),
        check_vma=False,
    )
```

profile of v0, /device:TPU:17, one launch (start us, length us, event | category | flops | bytes accessed | tf_op | source)
XLA Modules:
  0.0 108.6 jit_solution(15742423838032627012)
XLA Ops:
  0.6 0.7 fusion.178
  2.4 1.4 %scatter_custom_fusion = s32[512]{0:T(512)S(1)} fusion(s32[256]{0:T(256)S(1)} %compare_select_fusion.2, s32[256]{0:T(256)S(1)} %get-tuple-element.96, s32[]{:T(128)} %constant.177.clone.1), kind=kCustom, calls=%fused_computation.335 | custom fusion | bytes 2052 | tf_op jit(solution)/shard_map/scatter | solution.py:165
  3.8 0.7 all_to_all.9
  4.5 4.4 %all-to-all-start = ((s32[8,1,64]{2,1,0:T(1,128)}), s32[8,1,64]{2,1,0:T(1,128)S(1)}, u32[]{:S(2)}, u32[]{:S(2)}) async-start(s32[8,1,64]{2,1,0:T(1,128)} %all_to_all.9), calls=%async_computation | async-start | bytes 8192 | tf_op jit(solution)/shard_map/all_to_all | solution.py:170
  8.9 3.5 %collective-permute-start.1 = (f32[2,8,4,128]{3,2,1,0:T(4,128)S(1)}, f32[2,8,4,128]{3,2,1,0:T(4,128)S(1)}, u32[]{:S(2)}, u32[]{:S(2)}) collective-permute-start(f32[2,8,4,128]{3,2,1,0:T(4,128)S(1)} %get-tuple-element.85), channel_id=1, source_target_pairs={{0,8},{8,16},{16,24},{1,9},{9,17},{17,25},{2,10},{10,18},{18,26},{... | collective-permute-start | bytes 98312 | tf_op jit(solution)/shard_map/ppermute | solution.py:15
  12.5 1.9 %collective-permute-start = (f32[2,8,4,128]{3,2,1,0:T(4,128)S(1)}, f32[2,8,4,128]{3,2,1,0:T(4,128)S(1)}, u32[]{:S(2)}, u32[]{:S(2)}) collective-permute-start(f32[2,8,4,128]{3,2,1,0:T(4,128)S(1)} %get-tuple-element.86), channel_id=1, source_target_pairs={{8,0},{16,8},{24,16},{9,1},{17,9},{25,17},{10,2},{18,10},{26,18},{... | collective-permute-start | bytes 98312 | tf_op jit(solution)/shard_map/ppermute | solution.py:18
  14.8 0.6 copy-done.16
  15.9 1.2 %scatter_custom_fusion.1 = f32[512,2]{1,0:T(8,128)S(1)} fusion(s32[256]{0:T(256)S(1)} %compare_select_fusion.2, f32[256,2]{1,0:T(8,128)S(1)} %copy.28, f32[]{:T(128)} %constant.176.clone.1), kind=kCustom, calls=%fused_computation.67 | custom fusion | bytes 4100 | tf_op jit(solution)/shard_map/scatter | solution.py:159
  17.3 0.7 reshape.234
  18.0 4.3 %all-to-all-start.1 = ((f32[8,1,128]{2,1,0:T(1,128)}), f32[8,1,128]{2,1,0:T(1,128)S(1)}, u32[]{:S(2)}, u32[]{:S(2)}) async-start(f32[8,1,128]{2,1,0:T(1,128)} %reshape.234), calls=%async_computation.1 | async-start | bytes 8192 | tf_op jit(solution)/shard_map/all_to_all | solution.py:169
  22.8 0.7 reduce.17
  23.6 2.6 %all-to-all-done.1 = f32[8,1,128]{2,1,0:T(1,128)S(1)} async-done(((f32[8,1,128]{2,1,0:T(1,128)}), f32[8,1,128]{2,1,0:T(1,128)S(1)}, u32[]{:S(2)}, u32[]{:S(2)}) %all-to-all-start.1) | async-done | bytes 4128 | tf_op jit(solution)/shard_map/all_to_all | solution.py:169
  26.7 0.7 reduce.18
  27.6 2.4 %scatter_custom_fusion.2 = f32[2,1024]{0,1:T(8,128)S(1)} fusion(s32[512]{0:T(512)S(1)} %bitcast.139, f32[512,2]{1,0:T(8,128)S(1)} %bitcast.135, f32[]{:T(128)} %constant.176.clone.1), kind=kCustom, calls=%fused_computation.37 | custom fusion | flops 1024 | bytes 8196 | tf_op jit(solution)/shard_map/scatter-add | solution.py:175
  30.0 23.1 %psum.7 = f32[2,1024]{0,1:T(8,128)S(1)} all-reduce(f32[2,1024]{0,1:T(8,128)S(1)} %scatter_custom_fusion.2), channel_id=1, replica_groups=mesh['inl'=4,'xl'=2,'gz'=4] {'gz'}, use_global_device_ids=true, to_apply=%region_7.8 | all-reduce | flops 2048 | bytes 16384 | tf_op jit(solution)/shard_map/psum | solution.py:176
  53.8 2.1 %collective-permute-start.3 = (f32[2,8,16,4]{3,2,1,0:T(8,128)S(1)}, f32[2,8,16,4]{3,2,1,0:T(8,128)S(1)}, u32[]{:S(2)}, u32[]{:S(2)}) collective-permute-start(f32[2,8,16,4]{3,2,1,0:T(8,128)S(1)} %get-tuple-element.72), channel_id=1, source_target_pairs={{0,4},{1,5},{2,6},{3,7},{8,12},{9,13},{10,14},{11,15},{16,20},{17,... | collective-permute-start | bytes 12296 | tf_op jit(solution)/shard_map/ppermute | solution.py:15
  55.9 1.3 %collective-permute-start.2 = (f32[2,8,16,4]{3,2,1,0:T(8,128)S(1)}, f32[2,8,16,4]{3,2,1,0:T(8,128)S(1)}, u32[]{:S(2)}, u32[]{:S(2)}) collective-permute-start(f32[2,8,16,4]{3,2,1,0:T(8,128)S(1)} %get-tuple-element.73), channel_id=1, source_target_pairs={{4,0},{5,1},{6,2},{7,3},{12,8},{13,9},{14,10},{15,11},{20,16},{21,... | collective-permute-start | bytes 12296 | tf_op jit(solution)/shard_map/ppermute | solution.py:18
  57.8 3.8 %collective-permute-done.2 = f32[2,8,16,4]{3,2,1,0:T(8,128)S(1)} collective-permute-done((f32[2,8,16,4]{3,2,1,0:T(8,128)S(1)}, f32[2,8,16,4]{3,2,1,0:T(8,128)S(1)}, u32[]{:S(2)}, u32[]{:S(2)}) %collective-permute-start.2) | collective-permute-done | bytes 4128 | tf_op jit(solution)/shard_map/ppermute | solution.py:18
  61.9 2.1 %collective-permute-start.4 = (f32[2,4,16,136]{3,2,1,0:T(8,128)S(1)}, f32[2,4,16,136]{3,2,1,0:T(8,128)S(1)}, u32[]{:S(2)}, u32[]{:S(2)}) collective-permute-start(f32[2,4,16,136]{3,2,1,0:T(8,128)S(1)} %get-tuple-element.60), channel_id=1, source_target_pairs={{1,0},{2,1},{3,2},{5,4},{6,5},{7,6},{9,8},{10,9},{11,10},{13,12},{... | collective-permute-start | bytes 208904 | tf_op jit(solution)/shard_map/ppermute | solution.py:18
  63.9 3.2 %collective-permute-start.5 = (f32[2,4,16,136]{3,2,1,0:T(8,128)S(1)}, f32[2,4,16,136]{3,2,1,0:T(8,128)S(1)}, u32[]{:S(2)}, u32[]{:S(2)}) collective-permute-start(f32[2,4,16,136]{3,2,1,0:T(8,128)S(1)} %get-tuple-element.61), channel_id=1, source_target_pairs={{0,1},{1,2},{2,3},{4,5},{5,6},{6,7},{8,9},{9,10},{10,11},{12,13},{... | collective-permute-start | bytes 208904 | tf_op jit(solution)/shard_map/ppermute | solution.py:15
  67.9 2.3 %collective-permute-done.5 = f32[2,4,16,136]{3,2,1,0:T(8,128)S(1)} collective-permute-done((f32[2,4,16,136]{3,2,1,0:T(8,128)S(1)}, f32[2,4,16,136]{3,2,1,0:T(8,128)S(1)}, u32[]{:S(2)}, u32[]{:S(2)}) %collective-permute-start.5) | collective-permute-done | bytes 69664 | tf_op jit(solution)/shard_map/ppermute | solution.py:15
  71.0 0.6 add_subtract_fusion.1
  71.9 10.9 %collective-permute-start.7 = (f32[2,8,4,128]{3,2,1,0:T(4,128)S(1)}, f32[2,8,4,128]{3,2,1,0:T(4,128)S(1)}, u32[]{:S(2)}, u32[]{:S(2)}) collective-permute-start(f32[2,8,4,128]{3,2,1,0:T(4,128)S(1)} %get-tuple-element.76), channel_id=1, source_target_pairs={{0,8},{8,16},{16,24},{1,9},{9,17},{17,25},{2,10},{10,18},{18,26},{... | collective-permute-start | bytes 98312 | tf_op jit(solution)/shard_map/ppermute | solution.py:15
  82.9 1.9 %collective-permute-start.6 = (f32[2,8,4,128]{3,2,1,0:T(4,128)S(1)}, f32[2,8,4,128]{3,2,1,0:T(4,128)S(1)}, u32[]{:S(2)}, u32[]{:S(2)}) collective-permute-start(f32[2,8,4,128]{3,2,1,0:T(4,128)S(1)} %get-tuple-element.77), channel_id=1, source_target_pairs={{8,0},{16,8},{24,16},{9,1},{17,9},{25,17},{10,2},{18,10},{26,18},{... | collective-permute-start | bytes 98312 | tf_op jit(solution)/shard_map/ppermute | solution.py:18
  84.8 3.3 %collective-permute-done.6 = f32[2,8,4,128]{3,2,1,0:T(4,128)S(1)} collective-permute-done((f32[2,8,4,128]{3,2,1,0:T(4,128)S(1)}, f32[2,8,4,128]{3,2,1,0:T(4,128)S(1)}, u32[]{:S(2)}, u32[]{:S(2)}) %collective-permute-start.6) | collective-permute-done | bytes 32800 | tf_op jit(solution)/shard_map/ppermute | solution.py:18
  88.2 1.3 %collective-permute-start.9 = (f32[2,8,16,4]{3,2,1,0:T(8,128)S(1)}, f32[2,8,16,4]{3,2,1,0:T(8,128)S(1)}, u32[]{:S(2)}, u32[]{:S(2)}) collective-permute-start(f32[2,8,16,4]{3,2,1,0:T(8,128)S(1)} %get-tuple-element.68), channel_id=1, source_target_pairs={{0,4},{1,5},{2,6},{3,7},{8,12},{9,13},{10,14},{11,15},{16,20},{17,... | collective-permute-start | bytes 12296 | tf_op jit(solution)/shard_map/ppermute | solution.py:15
  89.5 1.3 %collective-permute-start.8 = (f32[2,8,16,4]{3,2,1,0:T(8,128)S(1)}, f32[2,8,16,4]{3,2,1,0:T(8,128)S(1)}, u32[]{:S(2)}, u32[]{:S(2)}) collective-permute-start(f32[2,8,16,4]{3,2,1,0:T(8,128)S(1)} %get-tuple-element.69), channel_id=1, source_target_pairs={{4,0},{5,1},{6,2},{7,3},{12,8},{13,9},{14,10},{15,11},{20,16},{21,... | collective-permute-start | bytes 12296 | tf_op jit(solution)/shard_map/ppermute | solution.py:18
  91.4 3.8 %collective-permute-done.8 = f32[2,8,16,4]{3,2,1,0:T(8,128)S(1)} collective-permute-done((f32[2,8,16,4]{3,2,1,0:T(8,128)S(1)}, f32[2,8,16,4]{3,2,1,0:T(8,128)S(1)}, u32[]{:S(2)}, u32[]{:S(2)}) %collective-permute-start.8) | collective-permute-done | bytes 4128 | tf_op jit(solution)/shard_map/ppermute | solution.py:18
  95.5 3.6 %collective-permute-start.10 = (f32[2,4,16,136]{3,2,1,0:T(8,128)S(1)}, f32[2,4,16,136]{3,2,1,0:T(8,128)S(1)}, u32[]{:S(2)}, u32[]{:S(2)}) collective-permute-start(f32[2,4,16,136]{3,2,1,0:T(8,128)S(1)} %get-tuple-element.58), channel_id=1, source_target_pairs={{1,0},{2,1},{3,2},{5,4},{6,5},{7,6},{9,8},{10,9},{11,10},{13,12},{... | collective-permute-start | bytes 208904 | tf_op jit(solution)/shard_map/ppermute | solution.py:18
  99.2 1.9 %collective-permute-start.11 = (f32[2,4,16,136]{3,2,1,0:T(8,128)S(1)}, f32[2,4,16,136]{3,2,1,0:T(8,128)S(1)}, u32[]{:S(2)}, u32[]{:S(2)}) collective-permute-start(f32[2,4,16,136]{3,2,1,0:T(8,128)S(1)} %get-tuple-element.59), channel_id=1, source_target_pairs={{0,1},{1,2},{2,3},{4,5},{5,6},{6,7},{8,9},{9,10},{10,11},{12,13},{... | collective-permute-start | bytes 208904 | tf_op jit(solution)/shard_map/ppermute | solution.py:15
  101.3 1.0 collective-permute-done.10
  102.3 4.2 %collective-permute-done.11 = f32[2,4,16,136]{3,2,1,0:T(8,128)S(1)} collective-permute-done((f32[2,4,16,136]{3,2,1,0:T(8,128)S(1)}, f32[2,4,16,136]{3,2,1,0:T(8,128)S(1)}, u32[]{:S(2)}, u32[]{:S(2)}) %collective-permute-start.11) | collective-permute-done | bytes 69664 | tf_op jit(solution)/shard_map/ppermute | solution.py:15
  (90 shorter events, 9.7 us)
Async XLA Ops:
  0.6 14.2 %copy-start = (f32[256,256]{1,0:T(8,128)S(1)}, f32[256,256]{1,0:T(8,128)}, u32[]{:S(2)}) copy-start(f32[256,256]{1,0:T(8,128)} %param.36) | copy-start | bytes 786436
  1.4 7.4 %copy-start.3 = (f32[8,8,128]{2,1,0:T(8,128)S(1)}, f32[8,8,128]{2,1,0:T(8,128)}, u32[]{:S(2)}) copy-start(f32[8,8,128]{2,1,0:T(8,128)} %param.25) | copy-start | bytes 98308
  1.4 7.4 %copy-start.4 = (f32[8,8,128]{2,1,0:T(8,128)S(1)}, f32[8,8,128]{2,1,0:T(8,128)}, u32[]{:S(2)}) copy-start(f32[8,8,128]{2,1,0:T(8,128)} %param.27) | copy-start | bytes 98308
  4.5 13.5 %all-to-all-start = ((s32[8,1,64]{2,1,0:T(1,128)}), s32[8,1,64]{2,1,0:T(1,128)S(1)}, u32[]{:S(2)}, u32[]{:S(2)}) async-start(s32[8,1,64]{2,1,0:T(1,128)} %all_to_all.9), calls=%async_computation | async-start | bytes 8192 | tf_op jit(solution)/shard_map/all_to_all | solution.py:170
  8.9 5.7 %copy-start.12 = (f32[8,8,128]{2,1,0:T(8,128)S(1)}, f32[8,8,128]{2,1,0:T(8,128)}, u32[]{:S(2)}) copy-start(f32[8,8,128]{2,1,0:T(8,128)} %param.33) | copy-start | bytes 98308
  8.9 5.7 %copy-start.13 = (f32[8,8,128]{2,1,0:T(8,128)S(1)}, f32[8,8,128]{2,1,0:T(8,128)}, u32[]{:S(2)}) copy-start(f32[8,8,128]{2,1,0:T(8,128)} %param.32) | copy-start | bytes 98308
  8.9 5.5 %copy-start.17 = (s32[256]{0:T(256)S(1)}, s32[256]{0:T(256)}, u32[]{:S(2)}) copy-start(s32[256]{0:T(256)} %param.41) | copy-start | bytes 3076
  8.9 5.5 %copy-start.18 = (f32[64]{0:T(128)S(1)}, f32[64]{0:T(128)}, u32[]{:S(2)}) copy-start(f32[64]{0:T(128)} %param.38) | copy-start | bytes 772
  8.9 44.7 %collective-permute-start.1 = (f32[2,8,4,128]{3,2,1,0:T(4,128)S(1)}, f32[2,8,4,128]{3,2,1,0:T(4,128)S(1)}, u32[]{:S(2)}, u32[]{:S(2)}) collective-permute-start(f32[2,8,4,128]{3,2,1,0:T(4,128)S(1)} %get-tuple-element.85), channel_id=1, source_target_pairs={{0,8},{8,16},{16,24},{1,9},{9,17},{17,25},{2,10},{10,18},{18,26},{... | collective-permute-start | bytes 98312 | tf_op jit(solution)/shard_map/ppermute | solution.py:15
  12.5 41.1 %collective-permute-start = (f32[2,8,4,128]{3,2,1,0:T(4,128)S(1)}, f32[2,8,4,128]{3,2,1,0:T(4,128)S(1)}, u32[]{:S(2)}, u32[]{:S(2)}) collective-permute-start(f32[2,8,4,128]{3,2,1,0:T(4,128)S(1)} %get-tuple-element.86), channel_id=1, source_target_pairs={{8,0},{16,8},{24,16},{9,1},{17,9},{25,17},{10,2},{18,10},{26,18},{... | collective-permute-start | bytes 98312 | tf_op jit(solution)/shard_map/ppermute | solution.py:18
  14.8 0.7 copy-start.16
  18.0 8.2 %all-to-all-start.1 = ((f32[8,1,128]{2,1,0:T(1,128)}), f32[8,1,128]{2,1,0:T(1,128)S(1)}, u32[]{:S(2)}, u32[]{:S(2)}) async-start(f32[8,1,128]{2,1,0:T(1,128)} %reshape.234), calls=%async_computation.1 | async-start | bytes 8192 | tf_op jit(solution)/shard_map/all_to_all | solution.py:169
  53.8 4.0 %collective-permute-start.3 = (f32[2,8,16,4]{3,2,1,0:T(8,128)S(1)}, f32[2,8,16,4]{3,2,1,0:T(8,128)S(1)}, u32[]{:S(2)}, u32[]{:S(2)}) collective-permute-start(f32[2,8,16,4]{3,2,1,0:T(8,128)S(1)} %get-tuple-element.72), channel_id=1, source_target_pairs={{0,4},{1,5},{2,6},{3,7},{8,12},{9,13},{10,14},{11,15},{16,20},{17,... | collective-permute-start | bytes 12296 | tf_op jit(solution)/shard_map/ppermute | solution.py:15
  55.9 5.7 %collective-permute-start.2 = (f32[2,8,16,4]{3,2,1,0:T(8,128)S(1)}, f32[2,8,16,4]{3,2,1,0:T(8,128)S(1)}, u32[]{:S(2)}, u32[]{:S(2)}) collective-permute-start(f32[2,8,16,4]{3,2,1,0:T(8,128)S(1)} %get-tuple-element.73), channel_id=1, source_target_pairs={{4,0},{5,1},{6,2},{7,3},{12,8},{13,9},{14,10},{15,11},{20,16},{21,... | collective-permute-start | bytes 12296 | tf_op jit(solution)/shard_map/ppermute | solution.py:18
  61.9 6.0 %collective-permute-start.4 = (f32[2,4,16,136]{3,2,1,0:T(8,128)S(1)}, f32[2,4,16,136]{3,2,1,0:T(8,128)S(1)}, u32[]{:S(2)}, u32[]{:S(2)}) collective-permute-start(f32[2,4,16,136]{3,2,1,0:T(8,128)S(1)} %get-tuple-element.60), channel_id=1, source_target_pairs={{1,0},{2,1},{3,2},{5,4},{6,5},{7,6},{9,8},{10,9},{11,10},{13,12},{... | collective-permute-start | bytes 208904 | tf_op jit(solution)/shard_map/ppermute | solution.py:18
  63.9 6.2 %collective-permute-start.5 = (f32[2,4,16,136]{3,2,1,0:T(8,128)S(1)}, f32[2,4,16,136]{3,2,1,0:T(8,128)S(1)}, u32[]{:S(2)}, u32[]{:S(2)}) collective-permute-start(f32[2,4,16,136]{3,2,1,0:T(8,128)S(1)} %get-tuple-element.61), channel_id=1, source_target_pairs={{0,1},{1,2},{2,3},{4,5},{5,6},{6,7},{8,9},{9,10},{10,11},{12,13},{... | collective-permute-start | bytes 208904 | tf_op jit(solution)/shard_map/ppermute | solution.py:15
  70.9 0.8 copy-start.5
  70.9 0.8 copy-start.6
  70.9 0.8 copy-start.7
  71.0 0.8 copy-start.8
  71.0 0.8 copy-start.9
  71.0 0.8 copy-start.14
  71.0 0.8 copy-start.15
  71.9 36.0 %copy-start.1 = (f32[8,8,128]{2,1,0:T(8,128)}, f32[8,8,128]{2,1,0:T(8,128)S(1)}, u32[]{:S(2)}) copy-start(f32[8,8,128]{2,1,0:T(8,128)S(1)} %get-tuple-element.94) | copy-start | bytes 98308
  71.9 36.0 %copy-start.2 = (f32[8,8,128]{2,1,0:T(8,128)}, f32[8,8,128]{2,1,0:T(8,128)S(1)}, u32[]{:S(2)}) copy-start(f32[8,8,128]{2,1,0:T(8,128)S(1)} %get-tuple-element.95) | copy-start | bytes 98308
  71.9 12.9 %collective-permute-start.7 = (f32[2,8,4,128]{3,2,1,0:T(4,128)S(1)}, f32[2,8,4,128]{3,2,1,0:T(4,128)S(1)}, u32[]{:S(2)}, u32[]{:S(2)}) collective-permute-start(f32[2,8,4,128]{3,2,1,0:T(4,128)S(1)} %get-tuple-element.76), channel_id=1, source_target_pairs={{0,8},{8,16},{16,24},{1,9},{9,17},{17,25},{2,10},{10,18},{18,26},{... | collective-permute-start | bytes 98312 | tf_op jit(solution)/shard_map/ppermute | solution.py:15
  82.9 5.2 %collective-permute-start.6 = (f32[2,8,4,128]{3,2,1,0:T(4,128)S(1)}, f32[2,8,4,128]{3,2,1,0:T(4,128)S(1)}, u32[]{:S(2)}, u32[]{:S(2)}) collective-permute-start(f32[2,8,4,128]{3,2,1,0:T(4,128)S(1)} %get-tuple-element.77), channel_id=1, source_target_pairs={{8,0},{16,8},{24,16},{9,1},{17,9},{25,17},{10,2},{18,10},{26,18},{... | collective-permute-start | bytes 98312 | tf_op jit(solution)/shard_map/ppermute | solution.py:18
  88.2 3.2 %collective-permute-start.9 = (f32[2,8,16,4]{3,2,1,0:T(8,128)S(1)}, f32[2,8,16,4]{3,2,1,0:T(8,128)S(1)}, u32[]{:S(2)}, u32[]{:S(2)}) collective-permute-start(f32[2,8,16,4]{3,2,1,0:T(8,128)S(1)} %get-tuple-element.68), channel_id=1, source_target_pairs={{0,4},{1,5},{2,6},{3,7},{8,12},{9,13},{10,14},{11,15},{16,20},{17,... | collective-permute-start | bytes 12296 | tf_op jit(solution)/shard_map/ppermute | solution.py:15
  89.5 5.7 %collective-permute-start.8 = (f32[2,8,16,4]{3,2,1,0:T(8,128)S(1)}, f32[2,8,16,4]{3,2,1,0:T(8,128)S(1)}, u32[]{:S(2)}, u32[]{:S(2)}) collective-permute-start(f32[2,8,16,4]{3,2,1,0:T(8,128)S(1)} %get-tuple-element.69), channel_id=1, source_target_pairs={{4,0},{5,1},{6,2},{7,3},{12,8},{13,9},{14,10},{15,11},{20,16},{21,... | collective-permute-start | bytes 12296 | tf_op jit(solution)/shard_map/ppermute | solution.py:18
  95.5 6.8 %collective-permute-start.10 = (f32[2,4,16,136]{3,2,1,0:T(8,128)S(1)}, f32[2,4,16,136]{3,2,1,0:T(8,128)S(1)}, u32[]{:S(2)}, u32[]{:S(2)}) collective-permute-start(f32[2,4,16,136]{3,2,1,0:T(8,128)S(1)} %get-tuple-element.58), channel_id=1, source_target_pairs={{1,0},{2,1},{3,2},{5,4},{6,5},{7,6},{9,8},{10,9},{11,10},{13,12},{... | collective-permute-start | bytes 208904 | tf_op jit(solution)/shard_map/ppermute | solution.py:18
  99.2 7.3 %collective-permute-start.11 = (f32[2,4,16,136]{3,2,1,0:T(8,128)S(1)}, f32[2,4,16,136]{3,2,1,0:T(8,128)S(1)}, u32[]{:S(2)}, u32[]{:S(2)}) collective-permute-start(f32[2,4,16,136]{3,2,1,0:T(8,128)S(1)} %get-tuple-element.59), channel_id=1, source_target_pairs={{0,1},{1,2},{2,3},{4,5},{5,6},{6,7},{8,9},{9,10},{10,11},{12,13},{... | collective-permute-start | bytes 208904 | tf_op jit(solution)/shard_map/ppermute | solution.py:15
  107.9 0.6 copy-start.11
  (1 other events, 0.6 us)
where the time goes:
time: 109 us
  starting transfers between devices  43.9 us (40%)
  blocking collectives  23.1 us (21%)
  waiting for transfers between devices  22.7 us (21%)
  other arithmetic  9.15 us (8%)
  local copies, waits for them, and re-layouts  8.32 us (8%)
  between operations  1.24 us (1%)
    psum x1, blocking collectives, local(): planes = lax.psum(planes, 'gz')  23.1 us
    ppermute x6, starting transfers between devices, with_halo(): lax.ppermute(lax.slice_in_dim(block, block.shape[dim] - width, None, axis...  23 us
    ppermute x6, waiting for transfers between devices, with_halo(): lax.ppermute(lax.slice_in_dim(block, 0, width, axis=dim), axis, backward)  12.4 us
    ppermute x6, starting transfers between devices, with_halo(): lax.ppermute(lax.slice_in_dim(block, 0, width, axis=dim), axis, backward)  12.1 us
    ppermute x6, waiting for transfers between devices, with_halo(): lax.ppermute(lax.slice_in_dim(block, block.shape[dim] - width, None, axis...  7.67 us
    all_to_all x1, starting transfers between devices, local(): lax.all_to_all(label_buffer, ('inl', 'xl'), split_axis=0, concat_axis=0,...  4.39 us
    all_to_all x1, starting transfers between devices, local(): lax.all_to_all(float_buffer, ('inl', 'xl'), split_axis=0, concat_axis=0,...  4.3 us
    all_to_all x1, waiting for transfers between devices, local(): lax.all_to_all(float_buffer, ('inl', 'xl'), split_axis=0, concat_axis=0,...  2.63 us
  transfers between devices with their start and end apart: 14, of which 10 were waited for; matrix products, arithmetic and copies ran while one was open for 8% of the time, Pallas kernels for 0%

commit v1 on v0

--- a/solution.py
+++ b/solution.py
@@ -173,7 +173,8 @@
     flat_labels = arrived_labels.reshape(-1)
     target = jnp.where(flat_labels >= 0, flat_labels, cells)
     planes = jnp.zeros((steps, cells), jnp.float32).at[:, target].add(amplitude.T, mode="drop")
-    planes = lax.psum(planes, "gz")
+    place_rows = lambda load, axis_tag: lax.all_gather(load, axis_tag).sum(axis=0)
+    planes = place_rows(planes, "gz")
     surface_flag = jnp.where(lax.axis_index("gz") == 0, 1.0, 0.0).astype(jnp.float32)
     planes = planes.reshape(steps, inline_cells, cross_cells) * surface_flag
     fields = (courant_square, thomsen_epsilon, thomsen_delta, shear_ratio, damping)

time: 109 us -> 92.6 us (0.85)
  blocking collectives: 23.1 us -> 8.74 us
  starting transfers between devices: 43.9 us -> 41.9 us
    psum x1 -> x0, blocking collectives: 23.1 us -> none  [local(): planes = lax.psum(planes, 'gz')]
    all_gather x0 -> x1, blocking collectives: none -> 8.74 us  [local(): lax.all_gather(load, axis_tag).sum(axis=0)]
    ppermute x6, starting transfers between devices: 23 us -> 20.9 us  [with_halo(): lax.ppermute(lax.slice_in_dim(block, block.shape[dim] - width, None, axis...]
    unnamed x40 -> x42, local copies, waits for them, and re-layouts: 2.27 us -> 2.69 us
  transfers between devices with their start and end apart: 14 -> 14, of which waited for: 10 -> 10; matrix products, arithmetic and copies ran while one was open for 8% -> 10% of each run, Pallas kernels for 0% -> 0%
where the time goes in v1:
time: 92.6 us; the launch traced here: 92 us
  starting transfers between devices  41.9 us (45%)
  waiting for transfers between devices  21.9 us (24%)
  other arithmetic  9.16 us (10%)
  local copies, waits for them, and re-layouts  8.74 us (9%)
  blocking collectives  8.74 us (9%)
  between operations  1.24 us (1%)
    ppermute x6, starting transfers between devices, with_halo(): lax.ppermute(lax.slice_in_dim(block, block.shape[dim] - width, None, axis...  20.9 us
    ppermute x6, waiting for transfers between devices, with_halo(): lax.ppermute(lax.slice_in_dim(block, 0, width, axis=dim), axis, backward)  12.7 us
    ppermute x6, starting transfers between devices, with_halo(): lax.ppermute(lax.slice_in_dim(block, 0, width, axis=dim), axis, backward)  12.3 us
    all_gather x1, blocking collectives, local(): lax.all_gather(load, axis_tag).sum(axis=0)  8.74 us
    ppermute x6, waiting for transfers between devices, with_halo(): lax.ppermute(lax.slice_in_dim(block, block.shape[dim] - width, None, axis...  6.63 us
    all_to_all x1, starting transfers between devices, local(): lax.all_to_all(label_buffer, ('inl', 'xl'), split_axis=0, concat_axis=0,...  4.39 us
    all_to_all x1, starting transfers between devices, local(): lax.all_to_all(float_buffer, ('inl', 'xl'), split_axis=0, concat_axis=0,...  4.3 us
    unnamed x42, local copies, waits for them, and re-layouts  2.69 us
  transfers between devices with their start and end apart: 14, of which 10 were waited for; matrix products, arithmetic and copies ran while one was open for 10% of the time, Pallas kernels for 0%

profile of v1, /device:TPU:17, one launch (start us, length us, event | category | flops | bytes accessed | tf_op | source)
XLA Modules:
  0.0 92.0 jit_solution(13974730886528725347)
XLA Ops:
  0.6 0.7 fusion.178
  2.4 1.4 %scatter_custom_fusion = s32[512]{0:T(512)S(1)} fusion(s32[256]{0:T(256)S(1)} %compare_select_fusion.2, s32[256]{0:T(256)S(1)} %get-tuple-element.96, s32[]{:T(128)} %constant.177.clone.1), kind=kCustom, calls=%fused_computation.335 | custom fusion | bytes 2052 | tf_op jit(solution)/shard_map/scatter | solution.py:165
  3.8 0.7 all_to_all.9
  4.5 4.4 %all-to-all-start = ((s32[8,1,64]{2,1,0:T(1,128)}), s32[8,1,64]{2,1,0:T(1,128)S(1)}, u32[]{:S(2)}, u32[]{:S(2)}) async-start(s32[8,1,64]{2,1,0:T(1,128)} %all_to_all.9), calls=%async_computation | async-start | bytes 8192 | tf_op jit(solution)/shard_map/all_to_all | solution.py:170
  8.9 3.5 %collective-permute-start.1 = (f32[2,8,4,128]{3,2,1,0:T(4,128)S(1)}, f32[2,8,4,128]{3,2,1,0:T(4,128)S(1)}, u32[]{:S(2)}, u32[]{:S(2)}) collective-permute-start(f32[2,8,4,128]{3,2,1,0:T(4,128)S(1)} %get-tuple-element.85), channel_id=1, source_target_pairs={{0,8},{8,16},{16,24},{1,9},{9,17},{17,25},{2,10},{10,18},{18,26},{... | collective-permute-start | bytes 98312 | tf_op jit(solution)/shard_map/ppermute | solution.py:15
  12.5 1.9 %collective-permute-start = (f32[2,8,4,128]{3,2,1,0:T(4,128)S(1)}, f32[2,8,4,128]{3,2,1,0:T(4,128)S(1)}, u32[]{:S(2)}, u32[]{:S(2)}) collective-permute-start(f32[2,8,4,128]{3,2,1,0:T(4,128)S(1)} %get-tuple-element.86), channel_id=1, source_target_pairs={{8,0},{16,8},{24,16},{9,1},{17,9},{25,17},{10,2},{18,10},{26,18},{... | collective-permute-start | bytes 98312 | tf_op jit(solution)/shard_map/ppermute | solution.py:18
  14.8 0.6 copy-done.16
  15.9 1.2 %scatter_custom_fusion.1 = f32[512,2]{1,0:T(8,128)S(1)} fusion(s32[256]{0:T(256)S(1)} %compare_select_fusion.2, f32[256,2]{1,0:T(8,128)S(1)} %copy.32, f32[]{:T(128)} %constant.176.clone.1), kind=kCustom, calls=%fused_computation.67 | custom fusion | bytes 4100 | tf_op jit(solution)/shard_map/scatter | solution.py:159
  17.3 0.7 reshape.238
  18.0 4.3 %all-to-all-start.1 = ((f32[8,1,128]{2,1,0:T(1,128)}), f32[8,1,128]{2,1,0:T(1,128)S(1)}, u32[]{:S(2)}, u32[]{:S(2)}) async-start(f32[8,1,128]{2,1,0:T(1,128)} %reshape.238), calls=%async_computation.1 | async-start | bytes 8192 | tf_op jit(solution)/shard_map/all_to_all | solution.py:169
  22.8 0.7 reduce.18
  23.6 2.6 %all-to-all-done.1 = f32[8,1,128]{2,1,0:T(1,128)S(1)} async-done(((f32[8,1,128]{2,1,0:T(1,128)}), f32[8,1,128]{2,1,0:T(1,128)S(1)}, u32[]{:S(2)}, u32[]{:S(2)}) %all-to-all-start.1) | async-done | bytes 4128 | tf_op jit(solution)/shard_map/all_to_all | solution.py:169
  26.7 0.7 reduce.19
  27.6 2.4 %scatter_custom_fusion.2 = f32[2,1024]{0,1:T(8,128)S(1)} fusion(s32[512]{0:T(512)S(1)} %bitcast.141, f32[512,2]{1,0:T(8,128)S(1)} %bitcast.137, f32[]{:T(128)} %constant.176.clone.1), kind=kCustom, calls=%fused_computation.37 | custom fusion | flops 1024 | bytes 8196 | tf_op jit(solution)/shard_map/scatter-add | solution.py:175
  30.2 8.7 %all-gather.1 = f32[4,2,1024]{2,1,0:T(2,128)S(1)} all-gather(f32[1,2,1024]{2,1,0:T(2,128)S(1)} %copy.36), channel_id=2, replica_groups=mesh['inl'=4,'xl'=2,'gz'=4] {'gz'}, dimensions={0}, use_global_device_ids=true | all-gather | bytes 40960 | tf_op jit(solution)/shard_map/all_gather | solution.py:176
  39.9 2.2 %collective-permute-start.3 = (f32[2,8,16,4]{3,2,1,0:T(8,128)S(1)}, f32[2,8,16,4]{3,2,1,0:T(8,128)S(1)}, u32[]{:S(2)}, u32[]{:S(2)}) collective-permute-start(f32[2,8,16,4]{3,2,1,0:T(8,128)S(1)} %get-tuple-element.72), channel_id=1, source_target_pairs={{0,4},{1,5},{2,6},{3,7},{8,12},{9,13},{10,14},{11,15},{16,20},{17,... | collective-permute-start | bytes 12296 | tf_op jit(solution)/shard_map/ppermute | solution.py:15
  42.1 1.3 %collective-permute-start.2 = (f32[2,8,16,4]{3,2,1,0:T(8,128)S(1)}, f32[2,8,16,4]{3,2,1,0:T(8,128)S(1)}, u32[]{:S(2)}, u32[]{:S(2)}) collective-permute-start(f32[2,8,16,4]{3,2,1,0:T(8,128)S(1)} %get-tuple-element.73), channel_id=1, source_target_pairs={{4,0},{5,1},{6,2},{7,3},{12,8},{13,9},{14,10},{15,11},{20,16},{21,... | collective-permute-start | bytes 12296 | tf_op jit(solution)/shard_map/ppermute | solution.py:18
  44.0 3.8 %collective-permute-done.2 = f32[2,8,16,4]{3,2,1,0:T(8,128)S(1)} collective-permute-done((f32[2,8,16,4]{3,2,1,0:T(8,128)S(1)}, f32[2,8,16,4]{3,2,1,0:T(8,128)S(1)}, u32[]{:S(2)}, u32[]{:S(2)}) %collective-permute-start.2) | collective-permute-done | bytes 4128 | tf_op jit(solution)/shard_map/ppermute | solution.py:18
  48.1 3.8 %collective-permute-start.4 = (f32[2,4,16,136]{3,2,1,0:T(8,128)S(1)}, f32[2,4,16,136]{3,2,1,0:T(8,128)S(1)}, u32[]{:S(2)}, u32[]{:S(2)}) collective-permute-start(f32[2,4,16,136]{3,2,1,0:T(8,128)S(1)} %get-tuple-element.60), channel_id=1, source_target_pairs={{1,0},{2,1},{3,2},{5,4},{6,5},{7,6},{9,8},{10,9},{11,10},{13,12},{... | collective-permute-start | bytes 208904 | tf_op jit(solution)/shard_map/ppermute | solution.py:18
  51.9 2.2 %collective-permute-start.5 = (f32[2,4,16,136]{3,2,1,0:T(8,128)S(1)}, f32[2,4,16,136]{3,2,1,0:T(8,128)S(1)}, u32[]{:S(2)}, u32[]{:S(2)}) collective-permute-start(f32[2,4,16,136]{3,2,1,0:T(8,128)S(1)} %get-tuple-element.61), channel_id=1, source_target_pairs={{0,1},{1,2},{2,3},{4,5},{5,6},{6,7},{8,9},{9,10},{10,11},{12,13},{... | collective-permute-start | bytes 208904 | tf_op jit(solution)/shard_map/ppermute | solution.py:15
  54.5 3.1 %collective-permute-done.5 = f32[2,4,16,136]{3,2,1,0:T(8,128)S(1)} collective-permute-done((f32[2,4,16,136]{3,2,1,0:T(8,128)S(1)}, f32[2,4,16,136]{3,2,1,0:T(8,128)S(1)}, u32[]{:S(2)}, u32[]{:S(2)}) %collective-permute-start.5) | collective-permute-done | bytes 69664 | tf_op jit(solution)/shard_map/ppermute | solution.py:15
  58.4 0.6 add_subtract_fusion.1
  59.3 8.5 %collective-permute-start.7 = (f32[2,8,4,128]{3,2,1,0:T(4,128)S(1)}, f32[2,8,4,128]{3,2,1,0:T(4,128)S(1)}, u32[]{:S(2)}, u32[]{:S(2)}) collective-permute-start(f32[2,8,4,128]{3,2,1,0:T(4,128)S(1)} %get-tuple-element.76), channel_id=1, source_target_pairs={{0,8},{8,16},{16,24},{1,9},{9,17},{17,25},{2,10},{10,18},{18,26},{... | collective-permute-start | bytes 98312 | tf_op jit(solution)/shard_map/ppermute | solution.py:15
  67.8 1.9 %collective-permute-start.6 = (f32[2,8,4,128]{3,2,1,0:T(4,128)S(1)}, f32[2,8,4,128]{3,2,1,0:T(4,128)S(1)}, u32[]{:S(2)}, u32[]{:S(2)}) collective-permute-start(f32[2,8,4,128]{3,2,1,0:T(4,128)S(1)} %get-tuple-element.77), channel_id=1, source_target_pairs={{8,0},{16,8},{24,16},{9,1},{17,9},{25,17},{10,2},{18,10},{26,18},{... | collective-permute-start | bytes 98312 | tf_op jit(solution)/shard_map/ppermute | solution.py:18
  69.8 3.3 %collective-permute-done.6 = f32[2,8,4,128]{3,2,1,0:T(4,128)S(1)} collective-permute-done((f32[2,8,4,128]{3,2,1,0:T(4,128)S(1)}, f32[2,8,4,128]{3,2,1,0:T(4,128)S(1)}, u32[]{:S(2)}, u32[]{:S(2)}) %collective-permute-start.6) | collective-permute-done | bytes 32800 | tf_op jit(solution)/shard_map/ppermute | solution.py:18
  73.2 1.3 %collective-permute-start.9 = (f32[2,8,16,4]{3,2,1,0:T(8,128)S(1)}, f32[2,8,16,4]{3,2,1,0:T(8,128)S(1)}, u32[]{:S(2)}, u32[]{:S(2)}) collective-permute-start(f32[2,8,16,4]{3,2,1,0:T(8,128)S(1)} %get-tuple-element.68), channel_id=1, source_target_pairs={{0,4},{1,5},{2,6},{3,7},{8,12},{9,13},{10,14},{11,15},{16,20},{17,... | collective-permute-start | bytes 12296 | tf_op jit(solution)/shard_map/ppermute | solution.py:15
  74.5 1.3 %collective-permute-start.8 = (f32[2,8,16,4]{3,2,1,0:T(8,128)S(1)}, f32[2,8,16,4]{3,2,1,0:T(8,128)S(1)}, u32[]{:S(2)}, u32[]{:S(2)}) collective-permute-start(f32[2,8,16,4]{3,2,1,0:T(8,128)S(1)} %get-tuple-element.69), channel_id=1, source_target_pairs={{4,0},{5,1},{6,2},{7,3},{12,8},{13,9},{14,10},{15,11},{20,16},{21,... | collective-permute-start | bytes 12296 | tf_op jit(solution)/shard_map/ppermute | solution.py:18
  76.4 3.8 %collective-permute-done.8 = f32[2,8,16,4]{3,2,1,0:T(8,128)S(1)} collective-permute-done((f32[2,8,16,4]{3,2,1,0:T(8,128)S(1)}, f32[2,8,16,4]{3,2,1,0:T(8,128)S(1)}, u32[]{:S(2)}, u32[]{:S(2)}) %collective-permute-start.8) | collective-permute-done | bytes 4128 | tf_op jit(solution)/shard_map/ppermute | solution.py:18
  80.5 2.1 %collective-permute-start.10 = (f32[2,4,16,136]{3,2,1,0:T(8,128)S(1)}, f32[2,4,16,136]{3,2,1,0:T(8,128)S(1)}, u32[]{:S(2)}, u32[]{:S(2)}) collective-permute-start(f32[2,4,16,136]{3,2,1,0:T(8,128)S(1)} %get-tuple-element.58), channel_id=1, source_target_pairs={{1,0},{2,1},{3,2},{5,4},{6,5},{7,6},{9,8},{10,9},{11,10},{13,12},{... | collective-permute-start | bytes 208904 | tf_op jit(solution)/shard_map/ppermute | solution.py:18
  82.6 3.2 %collective-permute-start.11 = (f32[2,4,16,136]{3,2,1,0:T(8,128)S(1)}, f32[2,4,16,136]{3,2,1,0:T(8,128)S(1)}, u32[]{:S(2)}, u32[]{:S(2)}) collective-permute-start(f32[2,4,16,136]{3,2,1,0:T(8,128)S(1)} %get-tuple-element.59), channel_id=1, source_target_pairs={{0,1},{1,2},{2,3},{4,5},{5,6},{6,7},{8,9},{9,10},{10,11},{12,13},{... | collective-permute-start | bytes 208904 | tf_op jit(solution)/shard_map/ppermute | solution.py:15
  86.0 1.6 %collective-permute-done.10 = f32[2,4,16,136]{3,2,1,0:T(8,128)S(1)} collective-permute-done((f32[2,4,16,136]{3,2,1,0:T(8,128)S(1)}, f32[2,4,16,136]{3,2,1,0:T(8,128)S(1)}, u32[]{:S(2)}, u32[]{:S(2)}) %collective-permute-start.10) | collective-permute-done | bytes 69664 | tf_op jit(solution)/shard_map/ppermute | solution.py:18
  87.6 2.4 %collective-permute-done.11 = f32[2,4,16,136]{3,2,1,0:T(8,128)S(1)} collective-permute-done((f32[2,4,16,136]{3,2,1,0:T(8,128)S(1)}, f32[2,4,16,136]{3,2,1,0:T(8,128)S(1)}, u32[]{:S(2)}, u32[]{:S(2)}) %collective-permute-start.11) | collective-permute-done | bytes 69664 | tf_op jit(solution)/shard_map/ppermute | solution.py:15
  (93 shorter events, 9.9 us)
Async XLA Ops:
  0.6 14.2 %copy-start = (f32[256,256]{1,0:T(8,128)S(1)}, f32[256,256]{1,0:T(8,128)}, u32[]{:S(2)}) copy-start(f32[256,256]{1,0:T(8,128)} %param.36) | copy-start | bytes 786436
  1.4 7.4 %copy-start.3 = (f32[8,8,128]{2,1,0:T(8,128)S(1)}, f32[8,8,128]{2,1,0:T(8,128)}, u32[]{:S(2)}) copy-start(f32[8,8,128]{2,1,0:T(8,128)} %param.25) | copy-start | bytes 98308
  1.4 7.4 %copy-start.4 = (f32[8,8,128]{2,1,0:T(8,128)S(1)}, f32[8,8,128]{2,1,0:T(8,128)}, u32[]{:S(2)}) copy-start(f32[8,8,128]{2,1,0:T(8,128)} %param.27) | copy-start | bytes 98308
  4.5 13.5 %all-to-all-start = ((s32[8,1,64]{2,1,0:T(1,128)}), s32[8,1,64]{2,1,0:T(1,128)S(1)}, u32[]{:S(2)}, u32[]{:S(2)}) async-start(s32[8,1,64]{2,1,0:T(1,128)} %all_to_all.9), calls=%async_computation | async-start | bytes 8192 | tf_op jit(solution)/shard_map/all_to_all | solution.py:170
  8.9 5.7 %copy-start.12 = (f32[8,8,128]{2,1,0:T(8,128)S(1)}, f32[8,8,128]{2,1,0:T(8,128)}, u32[]{:S(2)}) copy-start(f32[8,8,128]{2,1,0:T(8,128)} %param.33) | copy-start | bytes 98308
  8.9 5.7 %copy-start.13 = (f32[8,8,128]{2,1,0:T(8,128)S(1)}, f32[8,8,128]{2,1,0:T(8,128)}, u32[]{:S(2)}) copy-start(f32[8,8,128]{2,1,0:T(8,128)} %param.32) | copy-start | bytes 98308
  8.9 5.5 %copy-start.17 = (s32[256]{0:T(256)S(1)}, s32[256]{0:T(256)}, u32[]{:S(2)}) copy-start(s32[256]{0:T(256)} %param.41) | copy-start | bytes 3076
  8.9 5.5 %copy-start.18 = (f32[64]{0:T(128)S(1)}, f32[64]{0:T(128)}, u32[]{:S(2)}) copy-start(f32[64]{0:T(128)} %param.38) | copy-start | bytes 772
  8.9 30.8 %collective-permute-start.1 = (f32[2,8,4,128]{3,2,1,0:T(4,128)S(1)}, f32[2,8,4,128]{3,2,1,0:T(4,128)S(1)}, u32[]{:S(2)}, u32[]{:S(2)}) collective-permute-start(f32[2,8,4,128]{3,2,1,0:T(4,128)S(1)} %get-tuple-element.85), channel_id=1, source_target_pairs={{0,8},{8,16},{16,24},{1,9},{9,17},{17,25},{2,10},{10,18},{18,26},{... | collective-permute-start | bytes 98312 | tf_op jit(solution)/shard_map/ppermute | solution.py:15
  12.5 27.3 %collective-permute-start = (f32[2,8,4,128]{3,2,1,0:T(4,128)S(1)}, f32[2,8,4,128]{3,2,1,0:T(4,128)S(1)}, u32[]{:S(2)}, u32[]{:S(2)}) collective-permute-start(f32[2,8,4,128]{3,2,1,0:T(4,128)S(1)} %get-tuple-element.86), channel_id=1, source_target_pairs={{8,0},{16,8},{24,16},{9,1},{17,9},{25,17},{10,2},{18,10},{26,18},{... | collective-permute-start | bytes 98312 | tf_op jit(solution)/shard_map/ppermute | solution.py:18
  14.8 0.7 copy-start.16
  18.0 8.2 %all-to-all-start.1 = ((f32[8,1,128]{2,1,0:T(1,128)}), f32[8,1,128]{2,1,0:T(1,128)S(1)}, u32[]{:S(2)}, u32[]{:S(2)}) async-start(f32[8,1,128]{2,1,0:T(1,128)} %reshape.238), calls=%async_computation.1 | async-start | bytes 8192 | tf_op jit(solution)/shard_map/all_to_all | solution.py:169
  39.9 4.1 %collective-permute-start.3 = (f32[2,8,16,4]{3,2,1,0:T(8,128)S(1)}, f32[2,8,16,4]{3,2,1,0:T(8,128)S(1)}, u32[]{:S(2)}, u32[]{:S(2)}) collective-permute-start(f32[2,8,16,4]{3,2,1,0:T(8,128)S(1)} %get-tuple-element.72), channel_id=1, source_target_pairs={{0,4},{1,5},{2,6},{3,7},{8,12},{9,13},{10,14},{11,15},{16,20},{17,... | collective-permute-start | bytes 12296 | tf_op jit(solution)/shard_map/ppermute | solution.py:15
  42.1 5.7 %collective-permute-start.2 = (f32[2,8,16,4]{3,2,1,0:T(8,128)S(1)}, f32[2,8,16,4]{3,2,1,0:T(8,128)S(1)}, u32[]{:S(2)}, u32[]{:S(2)}) collective-permute-start(f32[2,8,16,4]{3,2,1,0:T(8,128)S(1)} %get-tuple-element.73), channel_id=1, source_target_pairs={{4,0},{5,1},{6,2},{7,3},{12,8},{13,9},{14,10},{15,11},{20,16},{21,... | collective-permute-start | bytes 12296 | tf_op jit(solution)/shard_map/ppermute | solution.py:18
  48.1 6.4 %collective-permute-start.4 = (f32[2,4,16,136]{3,2,1,0:T(8,128)S(1)}, f32[2,4,16,136]{3,2,1,0:T(8,128)S(1)}, u32[]{:S(2)}, u32[]{:S(2)}) collective-permute-start(f32[2,4,16,136]{3,2,1,0:T(8,128)S(1)} %get-tuple-element.60), channel_id=1, source_target_pairs={{1,0},{2,1},{3,2},{5,4},{6,5},{7,6},{9,8},{10,9},{11,10},{13,12},{... | collective-permute-start | bytes 208904 | tf_op jit(solution)/shard_map/ppermute | solution.py:18
  51.9 5.7 %collective-permute-start.5 = (f32[2,4,16,136]{3,2,1,0:T(8,128)S(1)}, f32[2,4,16,136]{3,2,1,0:T(8,128)S(1)}, u32[]{:S(2)}, u32[]{:S(2)}) collective-permute-start(f32[2,4,16,136]{3,2,1,0:T(8,128)S(1)} %get-tuple-element.61), channel_id=1, source_target_pairs={{0,1},{1,2},{2,3},{4,5},{5,6},{6,7},{8,9},{9,10},{10,11},{12,13},{... | collective-permute-start | bytes 208904 | tf_op jit(solution)/shard_map/ppermute | solution.py:15
  58.3 0.8 copy-start.5
  58.4 0.8 copy-start.6
  58.4 0.8 copy-start.7
  58.4 0.8 copy-start.8
  58.4 0.8 copy-start.9
  58.4 0.8 copy-start.14
  58.4 0.8 copy-start.15
  59.3 32.0 %copy-start.1 = (f32[8,8,128]{2,1,0:T(8,128)}, f32[8,8,128]{2,1,0:T(8,128)S(1)}, u32[]{:S(2)}) copy-start(f32[8,8,128]{2,1,0:T(8,128)S(1)} %get-tuple-element.94) | copy-start | bytes 98308
  59.3 32.0 %copy-start.2 = (f32[8,8,128]{2,1,0:T(8,128)}, f32[8,8,128]{2,1,0:T(8,128)S(1)}, u32[]{:S(2)}) copy-start(f32[8,8,128]{2,1,0:T(8,128)S(1)} %get-tuple-element.95) | copy-start | bytes 98308
  59.3 10.4 %collective-permute-start.7 = (f32[2,8,4,128]{3,2,1,0:T(4,128)S(1)}, f32[2,8,4,128]{3,2,1,0:T(4,128)S(1)}, u32[]{:S(2)}, u32[]{:S(2)}) collective-permute-start(f32[2,8,4,128]{3,2,1,0:T(4,128)S(1)} %get-tuple-element.76), channel_id=1, source_target_pairs={{0,8},{8,16},{16,24},{1,9},{9,17},{17,25},{2,10},{10,18},{18,26},{... | collective-permute-start | bytes 98312 | tf_op jit(solution)/shard_map/ppermute | solution.py:15
  67.8 5.2 %collective-permute-start.6 = (f32[2,8,4,128]{3,2,1,0:T(4,128)S(1)}, f32[2,8,4,128]{3,2,1,0:T(4,128)S(1)}, u32[]{:S(2)}, u32[]{:S(2)}) collective-permute-start(f32[2,8,4,128]{3,2,1,0:T(4,128)S(1)} %get-tuple-element.77), channel_id=1, source_target_pairs={{8,0},{16,8},{24,16},{9,1},{17,9},{25,17},{10,2},{18,10},{26,18},{... | collective-permute-start | bytes 98312 | tf_op jit(solution)/shard_map/ppermute | solution.py:18
  73.2 3.2 %collective-permute-start.9 = (f32[2,8,16,4]{3,2,1,0:T(8,128)S(1)}, f32[2,8,16,4]{3,2,1,0:T(8,128)S(1)}, u32[]{:S(2)}, u32[]{:S(2)}) collective-permute-start(f32[2,8,16,4]{3,2,1,0:T(8,128)S(1)} %get-tuple-element.68), channel_id=1, source_target_pairs={{0,4},{1,5},{2,6},{3,7},{8,12},{9,13},{10,14},{11,15},{16,20},{17,... | collective-permute-start | bytes 12296 | tf_op jit(solution)/shard_map/ppermute | solution.py:15
  74.5 5.7 %collective-permute-start.8 = (f32[2,8,16,4]{3,2,1,0:T(8,128)S(1)}, f32[2,8,16,4]{3,2,1,0:T(8,128)S(1)}, u32[]{:S(2)}, u32[]{:S(2)}) collective-permute-start(f32[2,8,16,4]{3,2,1,0:T(8,128)S(1)} %get-tuple-element.69), channel_id=1, source_target_pairs={{4,0},{5,1},{6,2},{7,3},{12,8},{13,9},{14,10},{15,11},{20,16},{21,... | collective-permute-start | bytes 12296 | tf_op jit(solution)/shard_map/ppermute | solution.py:18
  80.5 7.1 %collective-permute-start.10 = (f32[2,4,16,136]{3,2,1,0:T(8,128)S(1)}, f32[2,4,16,136]{3,2,1,0:T(8,128)S(1)}, u32[]{:S(2)}, u32[]{:S(2)}) collective-permute-start(f32[2,4,16,136]{3,2,1,0:T(8,128)S(1)} %get-tuple-element.58), channel_id=1, source_target_pairs={{1,0},{2,1},{3,2},{5,4},{6,5},{7,6},{9,8},{10,9},{11,10},{13,12},{... | collective-permute-start | bytes 208904 | tf_op jit(solution)/shard_map/ppermute | solution.py:18
  82.6 7.3 %collective-permute-start.11 = (f32[2,4,16,136]{3,2,1,0:T(8,128)S(1)}, f32[2,4,16,136]{3,2,1,0:T(8,128)S(1)}, u32[]{:S(2)}, u32[]{:S(2)}) collective-permute-start(f32[2,4,16,136]{3,2,1,0:T(8,128)S(1)} %get-tuple-element.59), channel_id=1, source_target_pairs={{0,1},{1,2},{2,3},{4,5},{5,6},{6,7},{8,9},{9,10},{10,11},{12,13},{... | collective-permute-start | bytes 208904 | tf_op jit(solution)/shard_map/ppermute | solution.py:15
  91.4 0.6 copy-start.10
  (1 other events, 0.6 us)
